TPU v7x, 256 devices: a whole 4x4x8 slice. The times are simulated.
256 devices in a mesh: chan: 64 (over z, y_hi, x), seg: 4 (over y_lo, core).
Axes of the slice: x: 4, y: 4 (y_hi: 2, y_lo: 2; y = y_hi * 2 + y_lo), z: 8, core: 2. Of those that a mesh axis runs over, the one named last changes fastest.
Arguments:
- spectra: bfloat16 [32, 128, 2, 8192], P(None, 'seg', None, 'chan'), may hold values from -6 to 6
- plan: int32 [4, 64], replicated, may hold values from 0 to 63, as said below
- assignment: int32 [8192], P('chan'), may hold values from 0 to 8191, as said below
Outputs:
- cross_spectra: float32 [4, 32, 2, 8192, 128], P(None, 'seg', None, 'chan')
Inputs may be any that keep to these rules, and one draw needn't show every extreme that they name: Each row is a pairing of the blocks: plan[r, plan[r, b]] = b and plan[r, b] != b; no two blocks are paired in two different rounds. `assignment`: entries b * 128 to (b + 1) * 128 - 1 are a permutation of that same range of channels.
All inputs are finite; a program needn't handle non-finite values.
Results may differ from a plain program's by a relative error of at most 0.0003.
Values may be sent and summed in bfloat16 or wider, within the bound.
No kernel may reach another device: no remote copies, remote signals or barrier semaphores. Data moves between devices by JAX's collectives and lax.ppermute only.
A program may use at most 128 MiB of HBM per device.

v0:
```python
import math
import jax
import jax.numpy as jnp
from jax import lax
from jax.sharding import PartitionSpec as P


def cross_block(own_rows, other_rows, chan_width):
    real_lhs = own_rows
    imag_lhs = jnp.stack([own_rows[:, :, 1], -own_rows[:, :, 0]], axis=2)
    lhs = jnp.stack([real_lhs, imag_lhs], axis=3)
    return jnp.einsum("fwkci,fwkj->fcij", lhs, other_rows, preferred_element_type=jnp.float32)


def on_device(spectra, plan, assignment):
    bin_count, win_local, _, chan_width = spectra.shape
    seg_count = lax.axis_size("seg")
    group_count = lax.axis_size("chan")
    win_count = win_local * seg_count
    scale = 1.0 / math.sqrt(win_count)
    local_slots = assignment - lax.axis_index("chan") * chan_width
    ordered = jnp.take(spectra, local_slots, axis=3)
    own_rows = lax.all_to_all(ordered, "seg", split_axis=0, concat_axis=1, tiled=True)
    my_bins = own_rows.shape[0]
    piece_rows = my_bins * win_count // group_count
    pieces = own_rows.reshape(group_count, piece_rows, 2 * chan_width)
    held = lax.all_to_all(pieces, "chan", split_axis=0, concat_axis=0, tiled=True)
    round_count = plan.shape[0]
    outgoing = jnp.take(held, plan.T, axis=0)
    arrived = lax.all_to_all(outgoing, "chan", split_axis=0, concat_axis=0, tiled=True)
    results = []
    for round_index in range(round_count):
        other_rows = arrived[:, round_index].reshape(my_bins, win_count, 2, chan_width)
        results.append(cross_block(own_rows, other_rows, chan_width) * scale)
    return jnp.stack(results)


def solution(mesh):
    in_specs = (P(None, "seg", None, "chan"), P(), P("chan"))
    out_specs = P(None, "seg", None, "chan", None)
    return jax.shard_map(
        on_device, mesh=mesh, in_specs=in_specs, out_specs=out_specs, check_vma=False
    )
```

profile of v0, /device:TPU:2, one launch (start us, length us, event | category | flops | bytes accessed | tf_op | source)
XLA Modules:
  0.0 130.8 jit_solution(9304834242603706841)
XLA Ops:
  0.0 0.7 compare_and_fusion.1
  0.7 3.5 %copy.30 = bf16[32,32,2,128]{1,0,2,3:T(8,128)(2,1)S(1)} copy(bf16[32,32,2,128]{3,2,1,0:T(2,128)(2,1)} %param.3) | data formatting | bytes 1048576 | tf_op args[0]
  4.1 2.1 %gather_fusion = bf16[128,32,32,2]{2,1,3,0:T(8,128)(2,1)} fusion(bf16[32,32,2,128]{1,0,2,3:T(8,128)(2,1)S(1)} %copy.30, s32[1024]{0:T(1024)S(1)} %pad_clamp_fusion.1), kind=kCustom, calls=%fused_computation | custom fusion | bytes 1049088 | tf_op jit(solution)/shard_map/jit(_take)/gather | solution.py:22
  6.3 1.9 %select_bitcast_fusion = bf16[32,32,2,128]{1,0,2,3:T(8,128)(2,1)S(1)} fusion(bf16[128,32,32,2]{2,1,3,0:T(8,128)(2,1)} %gather_fusion, pred[128]{0:T(512)(128)(4,1)S(1)} %get-tuple-element.5), kind=kLoop, calls=%fused_computation.3 | loop fusion | flops 262144 | bytes 1048704 | tf_op jit(solution)/shard_map/jit(_take)/select_n | solution.py:22
  8.1 2.1 %copy.31 = bf16[32,32,2,128]{3,1,2,0:T(8,128)(2,1)S(1)} copy(bf16[32,32,2,128]{1,0,2,3:T(8,128)(2,1)S(1)} %select_bitcast_fusion) | data formatting | bytes 1048576 | tf_op jit(solution)/shard_map/jit(_take)/select_n | solution.py:22
  10.2 11.5 %all_to_all.28 = bf16[32,32,2,128]{3,1,2,0:T(8,128)(2,1)S(1)} all-to-all(bf16[32,32,2,128]{3,1,2,0:T(8,128)(2,1)S(1)} %copy.31), channel_id=1, replica_groups=mesh['chan'=64,'seg'=4] {'seg'}, dimensions={0} | all-to-all | bytes 1048576 | tf_op jit(solution)/shard_map/all_to_all | solution.py:23
  21.7 0.5 copy.38
  22.3 1.1 reshape.15
  23.4 14.4 %all-to-all-start.1 = ((bf16[64,16,256]{2,1,0:T(8,128)(2,1)}), bf16[64,16,256]{2,1,0:T(8,128)(2,1)S(1)}, u32[]{:S(2)}, u32[]{:S(2)}) async-start(bf16[64,16,256]{2,1,0:T(8,128)(2,1)} %reshape.15), calls=%async_computation.1 | async-start | bytes 1048576 | tf_op jit(solution)/shard_map/all_to_all | solution.py:27
  37.8 0.1 copy.37
  37.9 0.1 copy.39
  38.0 0.1 reshape.26
  38.2 16.9 %all-to-all-done.1 = bf16[64,16,256]{2,1,0:T(8,128)(2,1)S(1)} async-done(((bf16[64,16,256]{2,1,0:T(8,128)(2,1)}), bf16[64,16,256]{2,1,0:T(8,128)(2,1)S(1)}, u32[]{:S(2)}, u32[]{:S(2)}) %all-to-all-start.1) | async-done | bytes 524320 | tf_op jit(solution)/shard_map/all_to_all | solution.py:27
  55.0 0.8 gather_fusion.1
  55.8 1.5 %broadcast_select_fusion = bf16[64,4,16,256]{3,2,1,0:T(8,128)(2,1)} fusion(bf16[64,4,16,256]{3,2,1,0:T(8,128)(2,1)S(1)} %bitcast.62, pred[64,4]{1,0:T(8,128)(4,1)S(1)} %copy.37), kind=kLoop, calls=%fused_computation.4 | loop fusion | flops 1048576 | bytes 4194560 | tf_op jit(solution)/shard_map/jit(_take)/select_n | solution.py:29
  57.3 7.4 %all-to-all-start.2 = ((bf16[64,4,16,256]{3,2,1,0:T(8,128)(2,1)}), bf16[64,4,16,256]{3,2,1,0:T(8,128)(2,1)S(1)}, u32[]{:S(2)}, u32[]{:S(2)}) async-start(bf16[64,4,16,256]{3,2,1,0:T(8,128)(2,1)} %broadcast_select_fusion), calls=%async_computation.2 | async-start | bytes 4194304 | tf_op jit(solution)/shard_map/all_to_all | solution.py:30
  64.8 1.0 copy.36
  65.9 0.2 copy.60
  66.1 0.2 copy.61
  66.3 0.1 neg.3
  66.3 0.8 maximum_bitcast_fusion
  67.2 47.6 %all-to-all-done.2 = bf16[64,4,16,256]{3,2,1,0:T(8,128)(2,1)S(1)} async-done(((bf16[64,4,16,256]{3,2,1,0:T(8,128)(2,1)}), bf16[64,4,16,256]{3,2,1,0:T(8,128)(2,1)S(1)}, u32[]{:S(2)}, u32[]{:S(2)}) %all-to-all-start.2) | async-done | bytes 2097184 | tf_op jit(solution)/shard_map/all_to_all | solution.py:30
  114.8 1.2 fusion.12
  116.0 2.1 %reshape_squeeze.12 = bf16[8,128,2,128]{3,2,1,0:T(2,128)(2,1)} reshape(bf16[64,1,16,256]{3,2,1,0:T(8,128)(2,1)} %get-tuple-element.7) | data formatting | bytes 1048576 | tf_op jit(solution)/shard_map/reshape;squeeze | solution.py:33
  118.0 2.0 %reshape_squeeze.15 = bf16[8,128,2,128]{3,2,1,0:T(2,128)(2,1)} reshape(bf16[64,1,16,256]{3,2,1,0:T(8,128)(2,1)} %get-tuple-element.8) | data formatting | bytes 1048576 | tf_op jit(solution)/shard_map/reshape;squeeze | solution.py:33
  120.0 1.6 %fusion.1 = f32[1,8,2,128,128]{4,3,2,1,0:T(8,128)S(1)} fusion(bf16[8,128,2,128,1]{3,2,1,0,4:T(2,128)(2,1)} %bitcast.67, bf16[8,128,2,1,128]{1,4,2,3,0:T(8,128)(2,1)S(1)} %copy-done.4, bf16[8,128,2,1,128]{1,4,2,3,0:T(8,128)(2,1)S(1)} %copy-done.1), kind=kOutput, calls=%fused_computation.10 | convolution fusion | flops 135004160 | bytes 2621440 | tf_op jit(solution)/shard_map/fwkci,fwkj->fcij/dot_general | solution.py:12
  121.6 0.4 fusion.7
  122.0 1.0 reshape_squeeze.14
  123.0 2.8 %fusion.5 = f32[1,8,2,128,128]{4,3,2,1,0:T(8,128)} fusion(bf16[8,128,2,128,1]{3,2,1,0,4:T(2,128)(2,1)} %bitcast.70, bf16[8,128,2,1,128]{1,4,2,3,0:T(8,128)(2,1)} %maximum_bitcast_fusion, bf16[8,128,2,1,128]{1,4,2,3,0:T(8,128)(2,1)} %copy.36), kind=kOutput, calls=%fused_computation.14 | convolution fusion | flops 135004160 | bytes 2621440 | tf_op jit(solution)/shard_map/fwkci,fwkj->fcij/dot_general | solution.py:12
  125.8 1.0 reshape_squeeze.13
  126.8 1.7 %fusion.3 = f32[1,8,2,128,128]{4,3,2,1,0:T(8,128)S(1)} fusion(bf16[8,128,2,128,1]{3,2,1,0,4:T(2,128)(2,1)} %bitcast.69, bf16[8,128,2,1,128]{1,4,2,3,0:T(8,128)(2,1)} %maximum_bitcast_fusion, bf16[8,128,2,1,128]{1,4,2,3,0:T(8,128)(2,1)S(1)} %copy-done.3), kind=kOutput, calls=%fused_computation.12 | convolution fusion | flops 135004160 | bytes 2621440 | tf_op jit(solution)/shard_map/fwkci,fwkj->fcij/dot_general | solution.py:12
  128.5 2.3 %pad_maximum_fusion = f32[4,8,2,128,128]{4,3,2,1,0:T(8,128)} fusion(f32[1,8,2,128,128]{4,3,2,1,0:T(8,128)S(1)} %fusion.7, f32[1,8,2,128,128]{4,3,2,1,0:T(8,128)S(1)} %copy-done, f32[1,8,2,128,128]{4,3,2,1,0:T(8,128)S(1)} %fusion.3, f32[1,8,2,128,128]{4,3,2,1,0:T(8,128)S(1)} %fusion.1), kind=kLoop, calls=%fused_computation.2 | loop fusion | flops 3145728 | bytes 8388608 | tf_op jit(solution)/shard_map/stack | solution.py:35
  (22 shorter events, 0.1 us)
Async XLA Ops:
  10.2 27.6 %copy-start.7 = (s32[4,64]{1,0:T(4,128)S(1)}, s32[4,64]{1,0:T(4,128)}, u32[]{:S(2)}) copy-start(s32[4,64]{1,0:T(4,128)} %param.4) | copy-start | bytes 3076
  23.4 31.6 %all-to-all-start.1 = ((bf16[64,16,256]{2,1,0:T(8,128)(2,1)}), bf16[64,16,256]{2,1,0:T(8,128)(2,1)S(1)}, u32[]{:S(2)}, u32[]{:S(2)}) async-start(bf16[64,16,256]{2,1,0:T(8,128)(2,1)} %reshape.15), calls=%async_computation.1 | async-start | bytes 1048576 | tf_op jit(solution)/shard_map/all_to_all | solution.py:27
  57.3 57.4 %all-to-all-start.2 = ((bf16[64,4,16,256]{3,2,1,0:T(8,128)(2,1)}), bf16[64,4,16,256]{3,2,1,0:T(8,128)(2,1)S(1)}, u32[]{:S(2)}, u32[]{:S(2)}) async-start(bf16[64,4,16,256]{3,2,1,0:T(8,128)(2,1)} %broadcast_select_fusion), calls=%async_computation.2 | async-start | bytes 4194304 | tf_op jit(solution)/shard_map/all_to_all | solution.py:30
  116.0 4.0 %copy-start.1 = (bf16[8,128,2,1,128]{1,4,2,3,0:T(8,128)(2,1)S(1)}, bf16[8,128,2,1,128]{1,4,2,3,0:T(8,128)(2,1)}, u32[]{:S(2)}) copy-start(bf16[8,128,2,1,128]{1,4,2,3,0:T(8,128)(2,1)} %copy.36) | copy-start | bytes 1572868
  116.0 4.0 %copy-start.4 = (bf16[8,128,2,1,128]{1,4,2,3,0:T(8,128)(2,1)S(1)}, bf16[8,128,2,1,128]{1,4,2,3,0:T(8,128)(2,1)}, u32[]{:S(2)}) copy-start(bf16[8,128,2,1,128]{1,4,2,3,0:T(8,128)(2,1)} %maximum_bitcast_fusion) | copy-start | bytes 1572868
  120.0 1.6 %copy-start.2 = (bf16[8,128,2,1,128]{1,4,2,3,0:T(8,128)(2,1)S(1)}, bf16[8,128,2,1,128]{1,4,2,3,0:T(8,128)(2,1)}, u32[]{:S(2)}) copy-start(bf16[8,128,2,1,128]{1,4,2,3,0:T(8,128)(2,1)} %copy.36) | copy-start | bytes 1572868
  120.0 1.6 %copy-start.5 = (bf16[8,128,2,1,128]{1,4,2,3,0:T(8,128)(2,1)S(1)}, bf16[8,128,2,1,128]{1,4,2,3,0:T(8,128)(2,1)}, u32[]{:S(2)}) copy-start(bf16[8,128,2,1,128]{1,4,2,3,0:T(8,128)(2,1)} %maximum_bitcast_fusion) | copy-start | bytes 1572868
  120.0 1.6 %copy-start.6 = (bf16[8,128,2,128]{3,2,1,0:T(2,128)(2,1)S(1)}, bf16[8,128,2,128]{3,2,1,0:T(2,128)(2,1)}, u32[]{:S(2)}) copy-start(bf16[8,128,2,128]{3,2,1,0:T(2,128)(2,1)} %reshape_squeeze.15) | copy-start | bytes 1572868
  123.0 3.8 %copy-start.3 = (bf16[8,128,2,1,128]{1,4,2,3,0:T(8,128)(2,1)S(1)}, bf16[8,128,2,1,128]{1,4,2,3,0:T(8,128)(2,1)}, u32[]{:S(2)}) copy-start(bf16[8,128,2,1,128]{1,4,2,3,0:T(8,128)(2,1)} %copy.36) | copy-start | bytes 1572868
  126.8 1.7 %copy-start = (f32[1,8,2,128,128]{4,3,2,1,0:T(8,128)S(1)}, f32[1,8,2,128,128]{4,3,2,1,0:T(8,128)}, u32[]{:S(2)}) copy-start(f32[1,8,2,128,128]{4,3,2,1,0:T(8,128)} %fusion.5) | copy-start | bytes 3145732
where the time goes:
time: 131 us
  waiting for transfers between devices  64.4 us (49%)
  starting transfers between devices  21.8 us (17%)
  local copies, waits for them, and re-layouts  19 us (15%)
  blocking collectives  11.5 us (9%)
  other arithmetic  7.26 us (6%)
  matrix products  6.52 us (5%)
    all_to_all x1, waiting for transfers between devices, on_device(): lax.all_to_all(outgoing, 'chan', split_axis=0, concat_axis=0, tiled=True)  47.6 us
    all_to_all x1, waiting for transfers between devices, on_device(): lax.all_to_all(pieces, 'chan', split_axis=0, concat_axis=0, tiled=True)  16.9 us
    all_to_all x1, starting transfers between devices, on_device(): lax.all_to_all(pieces, 'chan', split_axis=0, concat_axis=0, tiled=True)  14.4 us
    all_to_all x1, blocking collectives, on_device(): lax.all_to_all(ordered, 'seg', split_axis=0, concat_axis=1, tiled=True)  11.5 us
    all_to_all x1, starting transfers between devices, on_device(): lax.all_to_all(outgoing, 'chan', split_axis=0, concat_axis=0, tiled=True)  7.44 us
    dot_general x4, matrix products, cross_block(): jnp.einsum('fwkci,fwkj->fcij', lhs, other_rows, preferred_element_type=jn...  6.52 us
    another operation x4, local copies, waits for them, and re-layouts, on_device(): arrived[:, round_index].reshape(my_bins, win_count, 2, chan_width)  5.92 us
    unnamed x19, local copies, waits for them, and re-layouts  3.86 us
  transfers between devices with their start and end apart: 2, of which 2 were waited for; matrix products, arithmetic and copies ran while one was open for 2% of the time, Pallas kernels for 0%

commit v1 on v0

--- a/solution.py
+++ b/solution.py
@@ -20,7 +20,10 @@
     scale = 1.0 / math.sqrt(win_count)
     local_slots = assignment - lax.axis_index("chan") * chan_width
     ordered = jnp.take(spectra, local_slots, axis=3)
-    own_rows = lax.all_to_all(ordered, "seg", split_axis=0, concat_axis=1, tiled=True)
+    own_rows = jnp.concatenate(
+        lax.all_to_all(jnp.stack(jnp.split(ordered, lax.axis_size("seg"), axis=0)), "seg", 0, 0),
+        axis=1,
+    )
     my_bins = own_rows.shape[0]
     piece_rows = my_bins * win_count // group_count
     pieces = own_rows.reshape(group_count, piece_rows, 2 * chan_width)

time: 131 us -> 131 us (level)
    another operation x0 -> x6, local copies, waits for them, and re-layouts: none -> 3.28 us  [the longest x5 2.15 us: on_device(): jnp.stack(jnp.split(ordered, lax.axis_size('seg'), axis=0))]
    select_n x1 -> x0, local copies, waits for them, and re-layouts: 2.07 us -> none  [on_device(): ordered = jnp.take(spectra, local_slots, axis=3)]
where the time goes in v1:
time: 131 us
  waiting for transfers between devices  64.4 us (49%)
  starting transfers between devices  21.8 us (17%)
  local copies, waits for them, and re-layouts  19.1 us (15%)
  blocking collectives  11.5 us (9%)
  other arithmetic  7.33 us (6%)
  matrix products  6.52 us (5%)
    all_to_all x1, waiting for transfers between devices, on_device(): lax.all_to_all(outgoing, 'chan', split_axis=0, concat_axis=0, tiled=True)  47.6 us
    all_to_all x1, waiting for transfers between devices, on_device(): lax.all_to_all(pieces, 'chan', split_axis=0, concat_axis=0, tiled=True)  16.9 us
    all_to_all x1, starting transfers between devices, on_device(): lax.all_to_all(pieces, 'chan', split_axis=0, concat_axis=0, tiled=True)  14.4 us
    all_to_all x1, blocking collectives, on_device(): lax.all_to_all(jnp.stack(jnp.split(ordered, lax.axis_size('seg'), axis=0)...  11.5 us
    all_to_all x1, starting transfers between devices, on_device(): lax.all_to_all(outgoing, 'chan', split_axis=0, concat_axis=0, tiled=True)  7.44 us
    dot_general x4, matrix products, cross_block(): jnp.einsum('fwkci,fwkj->fcij', lhs, other_rows, preferred_element_type=jn...  6.52 us
    another operation x4, local copies, waits for them, and re-layouts, on_device(): arrived[:, round_index].reshape(my_bins, win_count, 2, chan_width)  5.93 us
    unnamed x19, local copies, waits for them, and re-layouts  3.86 us
  transfers between devices with their start and end apart: 2, of which 2 were waited for; matrix products, arithmetic and copies ran while one was open for 2% of the time, Pallas kernels for 0%

profile of v1, /device:TPU:2, one launch (start us, length us, event | category | flops | bytes accessed | tf_op | source)
XLA Modules:
  0.0 130.9 jit_solution(5096709436907361315)
XLA Ops:
  0.0 0.7 compare_and_fusion.1
  0.7 3.5 %copy.20 = bf16[32,32,2,128]{1,0,2,3:T(8,128)(2,1)S(1)} copy(bf16[32,32,2,128]{3,2,1,0:T(2,128)(2,1)} %param.3) | data formatting | bytes 1048576 | tf_op args[0]
  4.1 2.1 %gather_fusion = bf16[128,32,32,2]{2,1,3,0:T(8,128)(2,1)} fusion(bf16[32,32,2,128]{1,0,2,3:T(8,128)(2,1)S(1)} %copy.20, s32[1024]{0:T(1024)S(1)} %pad_clamp_fusion.1), kind=kCustom, calls=%fused_computation | custom fusion | bytes 1049088 | tf_op jit(solution)/shard_map/jit(_take)/gather | solution.py:22
  6.3 1.9 %select_bitcast_fusion = bf16[32,32,2,128]{1,0,2,3:T(8,128)(2,1)S(1)} fusion(bf16[128,32,32,2]{2,1,3,0:T(8,128)(2,1)} %gather_fusion, pred[128]{0:T(512)(128)(4,1)S(1)} %get-tuple-element.5), kind=kLoop, calls=%fused_computation.3 | loop fusion | flops 262144 | bytes 1048704 | tf_op jit(solution)/shard_map/jit(_take)/select_n | solution.py:22
  8.1 0.4 slice_bitcast_fusion.3
  8.5 0.4 copy.21
  9.0 0.4 copy.24
  9.4 0.4 copy.23
  9.9 0.4 copy.22
  10.4 11.5 %all_to_all.15 = bf16[4,8,32,2,128]{4,2,3,1,0:T(8,128)(2,1)S(1)} all-to-all(bf16[4,8,32,2,128]{4,2,3,1,0:T(8,128)(2,1)S(1)} %pad_maximum_fusion.2), channel_id=1, replica_groups=mesh['chan'=64,'seg'=4] {'seg'}, dimensions={0} | all-to-all | bytes 1048576 | tf_op jit(solution)/shard_map/all_to_all | solution.py:24
  21.9 0.5 copy.30
  22.4 1.1 reshape_reshape.3
  23.5 14.4 %all-to-all-start.1 = ((bf16[64,16,256]{2,1,0:T(8,128)(2,1)}), bf16[64,16,256]{2,1,0:T(8,128)(2,1)S(1)}, u32[]{:S(2)}, u32[]{:S(2)}) async-start(bf16[64,16,256]{2,1,0:T(8,128)(2,1)} %reshape_reshape.3), calls=%async_computation.1 | async-start | bytes 1048576 | tf_op jit(solution)/shard_map/all_to_all | solution.py:30
  38.3 16.9 %all-to-all-done.1 = bf16[64,16,256]{2,1,0:T(8,128)(2,1)S(1)} async-done(((bf16[64,16,256]{2,1,0:T(8,128)(2,1)}), bf16[64,16,256]{2,1,0:T(8,128)(2,1)S(1)}, u32[]{:S(2)}, u32[]{:S(2)}) %all-to-all-start.1) | async-done | bytes 524320 | tf_op jit(solution)/shard_map/all_to_all | solution.py:30
  55.2 0.8 gather_fusion.1
  55.9 1.5 %broadcast_select_fusion = bf16[64,4,16,256]{3,2,1,0:T(8,128)(2,1)} fusion(bf16[64,4,16,256]{3,2,1,0:T(8,128)(2,1)S(1)} %bitcast.71, pred[64,4]{1,0:T(8,128)(4,1)S(1)} %copy.29), kind=kLoop, calls=%fused_computation.4 | loop fusion | flops 1048576 | bytes 4194560 | tf_op jit(solution)/shard_map/jit(_take)/select_n | solution.py:32
  57.5 7.4 %all-to-all-start.2 = ((bf16[64,4,16,256]{3,2,1,0:T(8,128)(2,1)}), bf16[64,4,16,256]{3,2,1,0:T(8,128)(2,1)S(1)}, u32[]{:S(2)}, u32[]{:S(2)}) async-start(bf16[64,4,16,256]{3,2,1,0:T(8,128)(2,1)} %broadcast_select_fusion), calls=%async_computation.2 | async-start | bytes 4194304 | tf_op jit(solution)/shard_map/all_to_all | solution.py:33
  65.0 1.0 copy.28
  66.1 0.2 copy.53
  66.2 0.2 copy.54
  66.5 0.8 maximum_bitcast_fusion
  67.3 47.6 %all-to-all-done.2 = bf16[64,4,16,256]{3,2,1,0:T(8,128)(2,1)S(1)} async-done(((bf16[64,4,16,256]{3,2,1,0:T(8,128)(2,1)}), bf16[64,4,16,256]{3,2,1,0:T(8,128)(2,1)S(1)}, u32[]{:S(2)}, u32[]{:S(2)}) %all-to-all-start.2) | async-done | bytes 2097184 | tf_op jit(solution)/shard_map/all_to_all | solution.py:33
  114.9 1.2 fusion.12
  116.1 2.1 %reshape_squeeze.12 = bf16[8,128,2,128]{3,2,1,0:T(2,128)(2,1)} reshape(bf16[64,1,16,256]{3,2,1,0:T(8,128)(2,1)} %get-tuple-element.7) | data formatting | bytes 1048576 | tf_op jit(solution)/shard_map/reshape;squeeze | solution.py:36
  118.2 2.0 %reshape_squeeze.15 = bf16[8,128,2,128]{3,2,1,0:T(2,128)(2,1)} reshape(bf16[64,1,16,256]{3,2,1,0:T(8,128)(2,1)} %get-tuple-element.8) | data formatting | bytes 1048576 | tf_op jit(solution)/shard_map/reshape;squeeze | solution.py:36
  120.2 1.6 %fusion.1 = f32[1,8,2,128,128]{4,3,2,1,0:T(8,128)S(1)} fusion(bf16[8,128,2,128,1]{3,2,1,0,4:T(2,128)(2,1)} %bitcast.75, bf16[8,128,2,1,128]{1,4,2,3,0:T(8,128)(2,1)S(1)} %copy-done.4, bf16[8,128,2,1,128]{1,4,2,3,0:T(8,128)(2,1)S(1)} %copy-done.1), kind=kOutput, calls=%fused_computation.10 | convolution fusion | flops 135004160 | bytes 2621440 | tf_op jit(solution)/shard_map/fwkci,fwkj->fcij/dot_general | solution.py:12
  121.8 0.4 fusion.7
  122.2 1.0 reshape_squeeze.14
  123.2 2.8 %fusion.5 = f32[1,8,2,128,128]{4,3,2,1,0:T(8,128)} fusion(bf16[8,128,2,128,1]{3,2,1,0,4:T(2,128)(2,1)} %bitcast.78, bf16[8,128,2,1,128]{1,4,2,3,0:T(8,128)(2,1)} %maximum_bitcast_fusion, bf16[8,128,2,1,128]{1,4,2,3,0:T(8,128)(2,1)} %copy.28), kind=kOutput, calls=%fused_computation.14 | convolution fusion | flops 135004160 | bytes 2621440 | tf_op jit(solution)/shard_map/fwkci,fwkj->fcij/dot_general | solution.py:12
  126.0 1.0 reshape_squeeze.13
  126.9 1.7 %fusion.3 = f32[1,8,2,128,128]{4,3,2,1,0:T(8,128)S(1)} fusion(bf16[8,128,2,128,1]{3,2,1,0,4:T(2,128)(2,1)} %bitcast.77, bf16[8,128,2,1,128]{1,4,2,3,0:T(8,128)(2,1)} %maximum_bitcast_fusion, bf16[8,128,2,1,128]{1,4,2,3,0:T(8,128)(2,1)S(1)} %copy-done.3), kind=kOutput, calls=%fused_computation.12 | convolution fusion | flops 135004160 | bytes 2621440 | tf_op jit(solution)/shard_map/fwkci,fwkj->fcij/dot_general | solution.py:12
  128.7 2.3 %pad_maximum_fusion = f32[4,8,2,128,128]{4,3,2,1,0:T(8,128)} fusion(f32[1,8,2,128,128]{4,3,2,1,0:T(8,128)S(1)} %fusion.7, f32[1,8,2,128,128]{4,3,2,1,0:T(8,128)S(1)} %copy-done, f32[1,8,2,128,128]{4,3,2,1,0:T(8,128)S(1)} %fusion.3, f32[1,8,2,128,128]{4,3,2,1,0:T(8,128)S(1)} %fusion.1), kind=kLoop, calls=%fused_computation.2 | loop fusion | flops 3145728 | bytes 8388608 | tf_op jit(solution)/shard_map/stack | solution.py:38
  (27 shorter events, 0.6 us)
Async XLA Ops:
  10.4 27.6 %copy-start.7 = (s32[4,64]{1,0:T(4,128)S(1)}, s32[4,64]{1,0:T(4,128)}, u32[]{:S(2)}) copy-start(s32[4,64]{1,0:T(4,128)} %param.4) | copy-start | bytes 3076
  23.5 31.6 %all-to-all-start.1 = ((bf16[64,16,256]{2,1,0:T(8,128)(2,1)}), bf16[64,16,256]{2,1,0:T(8,128)(2,1)S(1)}, u32[]{:S(2)}, u32[]{:S(2)}) async-start(bf16[64,16,256]{2,1,0:T(8,128)(2,1)} %reshape_reshape.3), calls=%async_computation.1 | async-start | bytes 1048576 | tf_op jit(solution)/shard_map/all_to_all | solution.py:30
  57.5 57.4 %all-to-all-start.2 = ((bf16[64,4,16,256]{3,2,1,0:T(8,128)(2,1)}), bf16[64,4,16,256]{3,2,1,0:T(8,128)(2,1)S(1)}, u32[]{:S(2)}, u32[]{:S(2)}) async-start(bf16[64,4,16,256]{3,2,1,0:T(8,128)(2,1)} %broadcast_select_fusion), calls=%async_computation.2 | async-start | bytes 4194304 | tf_op jit(solution)/shard_map/all_to_all | solution.py:33
  116.1 4.0 %copy-start.1 = (bf16[8,128,2,1,128]{1,4,2,3,0:T(8,128)(2,1)S(1)}, bf16[8,128,2,1,128]{1,4,2,3,0:T(8,128)(2,1)}, u32[]{:S(2)}) copy-start(bf16[8,128,2,1,128]{1,4,2,3,0:T(8,128)(2,1)} %copy.28) | copy-start | bytes 1572868
  116.1 4.0 %copy-start.4 = (bf16[8,128,2,1,128]{1,4,2,3,0:T(8,128)(2,1)S(1)}, bf16[8,128,2,1,128]{1,4,2,3,0:T(8,128)(2,1)}, u32[]{:S(2)}) copy-start(bf16[8,128,2,1,128]{1,4,2,3,0:T(8,128)(2,1)} %maximum_bitcast_fusion) | copy-start | bytes 1572868
  120.1 1.6 %copy-start.2 = (bf16[8,128,2,1,128]{1,4,2,3,0:T(8,128)(2,1)S(1)}, bf16[8,128,2,1,128]{1,4,2,3,0:T(8,128)(2,1)}, u32[]{:S(2)}) copy-start(bf16[8,128,2,1,128]{1,4,2,3,0:T(8,128)(2,1)} %copy.28) | copy-start | bytes 1572868
  120.1 1.6 %copy-start.5 = (bf16[8,128,2,1,128]{1,4,2,3,0:T(8,128)(2,1)S(1)}, bf16[8,128,2,1,128]{1,4,2,3,0:T(8,128)(2,1)}, u32[]{:S(2)}) copy-start(bf16[8,128,2,1,128]{1,4,2,3,0:T(8,128)(2,1)} %maximum_bitcast_fusion) | copy-start | bytes 1572868
  120.1 1.6 %copy-start.6 = (bf16[8,128,2,128]{3,2,1,0:T(2,128)(2,1)S(1)}, bf16[8,128,2,128]{3,2,1,0:T(2,128)(2,1)}, u32[]{:S(2)}) copy-start(bf16[8,128,2,128]{3,2,1,0:T(2,128)(2,1)} %reshape_squeeze.15) | copy-start | bytes 1572868
  123.2 3.8 %copy-start.3 = (bf16[8,128,2,1,128]{1,4,2,3,0:T(8,128)(2,1)S(1)}, bf16[8,128,2,1,128]{1,4,2,3,0:T(8,128)(2,1)}, u32[]{:S(2)}) copy-start(bf16[8,128,2,1,128]{1,4,2,3,0:T(8,128)(2,1)} %copy.28) | copy-start | bytes 1572868
  126.9 1.7 %copy-start = (f32[1,8,2,128,128]{4,3,2,1,0:T(8,128)S(1)}, f32[1,8,2,128,128]{4,3,2,1,0:T(8,128)}, u32[]{:S(2)}) copy-start(f32[1,8,2,128,128]{4,3,2,1,0:T(8,128)} %fusion.5) | copy-start | bytes 3145732
